TPU v7x, 512 devices: a whole 4x8x8 slice. The times are simulated.
512 devices in a mesh: exp: 128 (over y, z, core), hid: 4 (over x).
Axes of the slice: x: 4, y: 8, z: 8, core: 2. Of those that a mesh axis runs over, the one named last changes fastest.
Arguments:
- tokens: bfloat16 [4096, 4096], P('exp', 'hid'), may hold values from -6 to 6
- expert_ids: int32 [4096, 8], P('exp'), may hold values from 0 to 127, all different within a row; in each aligned block of 16 rows (0 to 15, 16 to 31, ...) at most 2 rows name the same one
- combine: float32 [4096, 8], P('exp'), may hold values from 0.05 to 0.4
- sign_bits: int32 [128, 768], P('exp'), may hold values from 0 to 1
- w_gate: bfloat16 [128, 768, 4096], P('exp', 'hid'), may hold values from -0.09375 to 0.09375
- w_up: bfloat16 [128, 768, 4096], P('exp', 'hid'), may hold values from -0.09375 to 0.09375
- w_down: bfloat16 [128, 768, 4096], P('exp', 'hid'), may hold values from -0.21875 to 0.21875
Outputs:
- next_input: bfloat16 [4096, 4096], P('exp', 'hid')
- hessian: bfloat16 [128, 768, 768], P('exp', 'hid')
Inputs may be any that keep to these rules, and one draw needn't show every extreme that they name: `expert_ids`: each row names 8 different experts. Within each aligned block of 16 rows (one micro-batch of one index of exp) no expert is named by more than 2 rows, a bound that some block reaches. `sign_bits`: 0 stands for the sign -1, 1 for +1.
All inputs are finite; a program needn't handle non-finite values.
Results may differ from a plain program's by a relative error of at most 0.0065.
Values may be sent and summed in bfloat16 or wider, within the bound.
No kernel may reach another device: no remote copies, remote signals or barrier semaphores. Data moves between devices by JAX's collectives and lax.ppermute only.
A program may use at most 64 MiB of HBM per device.

v0:
```python
import jax
import jax.numpy as jnp
import numpy as np
from jax import lax
from jax.sharding import PartitionSpec as P


def paley_twelve():
    residues = set((number * number % 11 for number in range(1, 11)))
    legendre = [0] + [1 if number in residues else -1 for number in range(1, 11)]
    hadamard = np.zeros((12, 12))
    hadamard[0, 1:] = 1.0
    hadamard[1:, 0] = -1.0
    for row_index in range(11):
        for col_index in range(11):
            hadamard[row_index + 1, col_index + 1] = legendre[(col_index - row_index) % 11]
    return hadamard + np.eye(12)


def sylvester(order_size):
    positions = jnp.arange(order_size, dtype=jnp.int32)
    common = positions[:, None] & positions[None, :]
    parity = jnp.zeros_like(common)
    for bit_pos in range(order_size.bit_length()):
        parity = parity + (common >> bit_pos & 1)
    return (1 - 2 * (parity % 2)).astype(jnp.float32)


def rotate(hidden, sign_rows, paley_table, sylvester_table):
    values = hidden.astype(jnp.float32) * jnp.expand_dims(sign_rows, -2)
    blocks = values.reshape(values.shape[:-1] + (12, sylvester_table.shape[0]))
    turned = jnp.einsum(
        "...ab,ca,db->...cd", blocks, paley_table, sylvester_table, precision=lax.Precision.HIGHEST
    )
    return turned.reshape(values.shape)


def rank_of_pick(ids_block, experts):
    flat_ids = ids_block.reshape(-1)
    onehot = (flat_ids[:, None] == jnp.arange(experts, dtype=jnp.int32)[None, :]).astype(jnp.int32)
    before = jnp.cumsum(onehot, axis=0) - onehot
    return jnp.sum(before * onehot, axis=1).reshape(ids_block.shape)


def local(tokens, expert_ids, combine, sign_bits, w_gate, w_up, w_down):
    n_exp = lax.axis_size("exp")
    n_hid = lax.axis_size("hid")
    hid_index = lax.axis_index("hid")
    experts = w_gate.shape[0] * n_exp
    tok_rows, own_cols = tokens.shape
    half_rows = tok_rows // 2
    top_count = expert_ids.shape[1]
    capacity = min(half_rows, max(2, 2 * half_rows * top_count // experts))
    hidden_units = sign_bits.shape[1]
    share_rows = hidden_units // n_hid
    per_pair = 2 * capacity
    paley_table = jnp.asarray(paley_twelve(), jnp.float32)
    sylvester_table = sylvester(hidden_units // 12)
    sign_rows = (2 * sign_bits - 1).astype(jnp.float32)
    gram_scale = experts / (tok_rows * n_exp * top_count * hidden_units)
    down_parts = w_down[0].reshape(share_rows, n_hid, own_cols).transpose(1, 0, 2)
    down_cols = lax.all_to_all(down_parts, "hid", split_axis=0, concat_axis=0, tiled=True)
    down_cols = down_cols.reshape(hidden_units, own_cols)
    ranks = jnp.concatenate(
        [rank_of_pick(expert_ids[b * half_rows : (b + 1) * half_rows], experts) for b in range(2)],
        axis=0,
    )
    batch_of_row = (jnp.arange(tok_rows, dtype=jnp.int32) // half_rows)[:, None]
    target = expert_ids * per_pair + batch_of_row * capacity + ranks
    selector = jnp.any(
        target[None, :, :] == jnp.arange(experts * per_pair, dtype=jnp.int32)[:, None, None], axis=2
    ).astype(jnp.bfloat16)
    sending = jnp.dot(selector, tokens, preferred_element_type=jnp.float32).astype(jnp.bfloat16)
    arrived = lax.all_to_all(sending, "exp", split_axis=0, concat_axis=0, tiled=True)
    expert_in = lax.all_gather(arrived, "hid", axis=1, tiled=True)
    gate_act = jnp.dot(expert_in, w_gate[0].T, preferred_element_type=jnp.float32)
    up_act = jnp.dot(expert_in, w_up[0].T, preferred_element_type=jnp.float32)
    hidden = (jax.nn.silu(gate_act) * up_act).astype(jnp.bfloat16)
    full_hidden = lax.all_gather(hidden, "hid", axis=1, tiled=True)
    out_cols = jnp.dot(full_hidden, down_cols, preferred_element_type=jnp.float32).astype(
        jnp.bfloat16
    )
    back_rows = lax.all_to_all(out_cols, "exp", split_axis=0, concat_axis=0, tiled=True)
    picked = back_rows[target]
    mixed_rows = tokens.astype(jnp.float32) + jnp.sum(
        combine[:, :, None] * picked.astype(jnp.float32), axis=1
    )
    rotated = rotate(full_hidden, sign_rows[0], paley_table, sylvester_table)
    own_rotated = lax.dynamic_slice_in_dim(rotated, hid_index * share_rows, share_rows, 1)
    gram = jnp.dot(own_rotated.T, rotated, precision=lax.Precision.HIGHEST)
    hessian = (gram * gram_scale).astype(jnp.bfloat16)
    return (mixed_rows.astype(jnp.bfloat16), hessian[None])


def solution(mesh):
    placed = (
        P("exp", "hid"),
        P("exp", None),
        P("exp", None),
        P("exp", None),
        P("exp", "hid", None),
        P("exp", "hid", None),
        P("exp", "hid", None),
    )
    return jax.shard_map(
        local,
        mesh=mesh,
        in_specs=placed,
        out_specs=(P("exp", "hid"), P("exp", "hid", None)),
        check_vma=False,
    )
```

profile of v0, /device:TPU:1, one launch (start us, length us, event | category | flops | bytes accessed | tf_op | source)
XLA Modules:
  0.0 198.2 jit_solution(3465828189842515196)
XLA Ops:
  7.2 0.9 fusion.46
  9.7 0.8 compare_select_fusion
  10.8 1.3 convolution_convert_fusion.1
  12.1 1.2 all_to_all.19
  13.3 48.9 %all_to_all.29 = bf16[128,4,1024]{2,1,0:T(4,128)(2,1)S(1)} all-to-all(bf16[128,4,1024]{2,1,0:T(4,128)(2,1)} %all_to_all.19), channel_id=1, replica_groups=mesh['exp'=128,'hid'=4] {'exp'}, dimensions={0} | all-to-all | bytes 2097152 | tf_op jit(solution)/shard_map/all_to_all | solution.py:74
  62.2 1.1 all_to_all.21
  63.3 2.9 %reshape_squeeze.3 = bf16[192,4,1024]{2,1,0:T(4,128)(2,1)S(1)} reshape(bf16[1,192,4096]{2,1,0:T(8,128)(2,1)} %param.14) | data formatting | bytes 3145728 | tf_op jit(solution)/shard_map/reshape;squeeze | solution.py:61
  66.2 1.7 copy.41
  67.9 4.3 %all-to-all-start.1 = ((bf16[4,192,1024]{2,1,0:T(8,128)(2,1)}), bf16[4,192,1024]{2,1,0:T(8,128)(2,1)}, u32[]{:S(2)}, u32[]{:S(2)}) async-start(bf16[4,192,1024]{2,1,0:T(8,128)(2,1)} %copy.41), calls=%async_computation.1 | async-start | bytes 3145728 | tf_op jit(solution)/shard_map/all_to_all | solution.py:62
  72.2 54.8 %all-gather.2.cloned.1.call-done = bf16[512,4096]{1,0:T(8,128)(2,1)} async-done(((bf16[512,1024]{1,0:T(8,128)(2,1)}), bf16[512,4096]{1,0:T(8,128)(2,1)}) %all-gather.2.cloned.1.call-update) | async-done | bytes 4194320 | tf_op jit(solution)/shard_map/all_gather | solution.py:75
  127.0 3.9 %fusion.4 = f32[512,192]{0,1:T(8,128)S(1)} fusion(bf16[512,4096]{1,0:T(8,128)(2,1)} %all-gather.2.cloned.1.call-done, bf16[1,192,4096]{2,1,0:T(8,128)(2,1)S(1)} %copy-done), kind=kOutput, calls=%fused_computation.5 | convolution fusion | flops 805306368 | bytes 6160384 | tf_op jit(solution)/shard_map/dot_general | solution.py:76
  130.9 1.5 fusion.12
  132.4 10.4 %all_gather.7 = bf16[512,768]{0,1:T(8,128)(2,1)S(1)} all-gather(bf16[512,192]{0,1:T(8,128)(2,1)S(1)} %fusion.12), channel_id=1, replica_groups=mesh['exp'=128,'hid'=4] {'hid'}, dimensions={1}, use_global_device_ids=true | all-gather | bytes 983040 | tf_op jit(solution)/shard_map/all_gather | solution.py:79
  142.8 2.4 %convolution_convert_fusion = bf16[512,1024]{1,0:T(8,128)(2,1)S(1)} fusion(bf16[512,768]{0,1:T(8,128)(2,1)S(1)} %all_gather.7, bf16[768,1024]{1,0:T(8,128)(2,1)} %bitcast.3), kind=kOutput, calls=%fused_computation.10 | convolution fusion | flops 805830656 | bytes 3407872 | tf_op jit(solution)/shard_map/dot_general | solution.py:80
  145.3 1.3 all_to_all.23
  146.5 11.1 %all-to-all-start.2 = ((bf16[128,4,1024]{2,1,0:T(4,128)(2,1)}), bf16[128,4,1024]{2,1,0:T(4,128)(2,1)}, u32[]{:S(2)}, u32[]{:S(2)}) async-start(bf16[128,4,1024]{2,1,0:T(4,128)(2,1)} %all_to_all.23), calls=%async_computation.2 | async-start | bytes 2097152 | tf_op jit(solution)/shard_map/all_to_all | solution.py:83
  158.4 2.6 %fusion = f32[12,512,64]{1,0,2:T(8,128)S(1)} fusion(f32[12,12,1]{1,0,2:T(8,128)S(1)} %copy-done.2, f32[512,12,64]{0,2,1:T(8,128)S(1)} %bitcast.33), kind=kOutput, calls=%fused_computation.1 | convolution fusion | flops 56623104 | bytes 3146304 | tf_op jit(solution)/shard_map/...ab,ca,db->...cd/dot_general | solution.py:32
  161.0 2.5 %fusion.6 = f32[12,512,64]{1,2,0:T(8,128)S(1)} fusion(f32[12,512,64]{1,0,2:T(8,128)S(1)} %fusion), kind=kOutput, calls=%fused_computation.7 | convolution fusion | flops 302133248 | bytes 3145728 | tf_op jit(solution)/shard_map/...ab,ca,db->...cd/dot_general | solution.py:32
  163.5 2.4 %fusion.15 = bf16[1,192,768]{2,1,0:T(8,128)(2,1)} fusion(f32[512,768]{0,1:T(8,128)S(1)} %bitcast.34, s32[]{:T(128)S(6)} %select_n.25), kind=kOutput, calls=%fused_computation.16 | convolution fusion | flops 906264576 | bytes 2260996 | tf_op jit(solution)/shard_map/dot_general | solution.py:90
  166.0 21.8 %all-to-all-done.2 = bf16[128,4,1024]{2,1,0:T(4,128)(2,1)} async-done(((bf16[128,4,1024]{2,1,0:T(4,128)(2,1)}), bf16[128,4,1024]{2,1,0:T(4,128)(2,1)}, u32[]{:S(2)}, u32[]{:S(2)}) %all-to-all-start.2) | async-done | bytes 1048608 | tf_op jit(solution)/shard_map/all_to_all | solution.py:83
  187.8 1.3 all_to_all.25
  189.1 1.2 gather_fusion
  190.3 0.4 fusion.16
  190.7 0.6 add_convert_fusion
  (40 shorter events, 2.6 us)
Async XLA Ops:
  7.2 119.8 %copy-start = (bf16[1,192,4096]{2,1,0:T(8,128)(2,1)S(1)}, bf16[1,192,4096]{2,1,0:T(8,128)(2,1)}, u32[]{:S(2)}) copy-start(bf16[1,192,4096]{2,1,0:T(8,128)(2,1)} %param.12) | copy-start | bytes 4718596
  7.2 119.8 %all-gather.2.cloned.1.call-start = ((), (), s32[]{:S(2)}) async-start(), calls=%async_computation.3 | async-start | bytes 5242880 | tf_op jit(solution)/shard_map/all_gather | solution.py:75
  67.9 75.0 %all-to-all-start.1 = ((bf16[4,192,1024]{2,1,0:T(8,128)(2,1)}), bf16[4,192,1024]{2,1,0:T(8,128)(2,1)}, u32[]{:S(2)}, u32[]{:S(2)}) async-start(bf16[4,192,1024]{2,1,0:T(8,128)(2,1)} %copy.41), calls=%async_computation.1 | async-start | bytes 3145728 | tf_op jit(solution)/shard_map/all_to_all | solution.py:62
  72.2 58.6 %copy-start.6 = (bf16[1,192,4096]{2,1,0:T(8,128)(2,1)S(1)}, bf16[1,192,4096]{2,1,0:T(8,128)(2,1)}, u32[]{:S(2)}) copy-start(bf16[1,192,4096]{2,1,0:T(8,128)(2,1)} %param.13) | copy-start | bytes 4718596
  127.0 3.9 %copy-start.5 = (bf16[512,4096]{1,0:T(8,128)(2,1)S(1)}, bf16[512,4096]{1,0:T(8,128)(2,1)}, u32[]{:S(2)}) copy-start(bf16[512,4096]{1,0:T(8,128)(2,1)} %all-gather.2.cloned.1.call-done) | copy-start | bytes 12582916
  146.5 11.3 %copy-start.3 = (f32[32,8]{0,1:T(8,128)S(1)}, f32[32,8]{0,1:T(8,128)}, u32[]{:S(2)}) copy-start(f32[32,8]{0,1:T(8,128)} %param.10) | copy-start | bytes 3076
  146.5 11.4 %copy-start.4 = (s32[1,768]{1,0:T(1,128)S(1)}, s32[1,768]{1,0:T(1,128)}, u32[]{:S(2)}) copy-start(s32[1,768]{1,0:T(1,128)} %param.11) | copy-start | bytes 9220
  146.5 41.2 %all-to-all-start.2 = ((bf16[128,4,1024]{2,1,0:T(4,128)(2,1)}), bf16[128,4,1024]{2,1,0:T(4,128)(2,1)}, u32[]{:S(2)}, u32[]{:S(2)}) async-start(bf16[128,4,1024]{2,1,0:T(4,128)(2,1)} %all_to_all.23), calls=%async_computation.2 | async-start | bytes 2097152 | tf_op jit(solution)/shard_map/all_to_all | solution.py:83
  157.7 0.7 copy-start.2
  189.1 1.6 copy-start.1
Sparse Core Ops, SparseCore 0:
  63.4 63.5 all-gather.1
where the time goes:
time: 199 us; the launch traced here: 198 us
  waiting for transfers between devices  76.6 us (38%)
  blocking collectives  59.3 us (30%)
  matrix products  16.7 us (8%)
  starting transfers between devices  15.5 us (8%)
  between operations  14.3 us (7%)
  local copies, waits for them, and re-layouts  12.7 us (6%)
  other arithmetic  3.08 us (2%)
    all_gather x1, waiting for transfers between devices, local(): expert_in = lax.all_gather(arrived, 'hid', axis=1, tiled=True)  54.8 us
    all_to_all x1, blocking collectives, local(): lax.all_to_all(sending, 'exp', split_axis=0, concat_axis=0, tiled=True)  48.9 us
    all_to_all x1, waiting for transfers between devices, local(): lax.all_to_all(out_cols, 'exp', split_axis=0, concat_axis=0, tiled=True)  21.8 us
    all_to_all x1, starting transfers between devices, local(): lax.all_to_all(out_cols, 'exp', split_axis=0, concat_axis=0, tiled=True)  11.1 us
    all_gather x1, blocking collectives, local(): full_hidden = lax.all_gather(hidden, 'hid', axis=1, tiled=True)  10.4 us
    dot_general x2, matrix products, rotate(): jnp.einsum('...ab,ca,db->...cd', blocks, paley_table, sylvester_table, pr...  5.15 us
    all_to_all x1, starting transfers between devices, local(): lax.all_to_all(down_parts, 'hid', split_axis=0, concat_axis=0, tiled=True)  4.35 us
  transfers between devices with their start and end apart: 3, of which 2 were waited for; matrix products, arithmetic and copies ran while one was open for 9% of the time, Pallas kernels for 0%

commit v1 on v0

--- a/solution.py
+++ b/solution.py
@@ -72,7 +72,9 @@
     ).astype(jnp.bfloat16)
     sending = jnp.dot(selector, tokens, preferred_element_type=jnp.float32).astype(jnp.bfloat16)
     arrived = lax.all_to_all(sending, "exp", split_axis=0, concat_axis=0, tiled=True)
-    expert_in = lax.all_gather(arrived, "hid", axis=1, tiled=True)
+    expert_in = jnp.concatenate(
+        lax.all_to_all(jnp.stack([arrived] * lax.axis_size("hid")), "hid", 0, 0), axis=1
+    )
     gate_act = jnp.dot(expert_in, w_gate[0].T, preferred_element_type=jnp.float32)
     up_act = jnp.dot(expert_in, w_up[0].T, preferred_element_type=jnp.float32)
     hidden = (jax.nn.silu(gate_act) * up_act).astype(jnp.bfloat16)

time: 199 us -> 195 us (0.980)
  between operations: 14.3 us -> 0.88 us
  waiting for transfers between devices: 76.6 us -> 64.4 us
  blocking collectives: 59.3 us -> 68.2 us
  starting transfers between devices: 15.5 us -> 23.6 us
  local copies, waits for them, and re-layouts: 12.7 us -> 16.6 us
    all_gather x1 -> x0, waiting for transfers between devices: 54.8 us -> none  [local(): expert_in = lax.all_gather(arrived, 'hid', axis=1, tiled=True)]
    all_to_all x0 -> x1, waiting for transfers between devices: none -> 42.6 us  [local(): lax.all_to_all(jnp.stack([arrived] * lax.axis_size('hid')), 'hid', 0, 0)]
    all_gather x1, blocking collectives: 10.4 us -> 19.3 us  [local(): full_hidden = lax.all_gather(hidden, 'hid', axis=1, tiled=True)]
    another operation x0 -> x3, local copies, waits for them, and re-layouts: none -> 4.91 us  [local(): jnp.stack([arrived] * lax.axis_size('hid'))]
    all_to_all x0 -> x1, starting transfers between devices: none -> 4.86 us  [local(): lax.all_to_all(jnp.stack([arrived] * lax.axis_size('hid')), 'hid', 0, 0)]
    all_to_all x1, starting transfers between devices: 11.1 us -> 14.3 us  [local(): lax.all_to_all(out_cols, 'exp', split_axis=0, concat_axis=0, tiled=True)]
  transfers between devices with their start and end apart: 3 -> 3, of which waited for: 2 -> 2; matrix products, arithmetic and copies ran while one was open for 9% -> 10% of each run, Pallas kernels for 0% -> 0%
where the time goes in v1:
time: 195 us; the launch traced here: 194 us
  blocking collectives  68.2 us (35%)
  waiting for transfers between devices  64.4 us (33%)
  starting transfers between devices  23.6 us (12%)
  matrix products  17.8 us (9%)
  local copies, waits for them, and re-layouts  16.6 us (9%)
  other arithmetic  3.08 us (2%)
    all_to_all x1, blocking collectives, local(): lax.all_to_all(sending, 'exp', split_axis=0, concat_axis=0, tiled=True)  48.9 us
    all_to_all x1, waiting for transfers between devices, local(): lax.all_to_all(jnp.stack([arrived] * lax.axis_size('hid')), 'hid', 0, 0)  42.6 us
    all_to_all x1, waiting for transfers between devices, local(): lax.all_to_all(out_cols, 'exp', split_axis=0, concat_axis=0, tiled=True)  21.8 us
    all_gather x1, blocking collectives, local(): full_hidden = lax.all_gather(hidden, 'hid', axis=1, tiled=True)  19.3 us
    all_to_all x1, starting transfers between devices, local(): lax.all_to_all(out_cols, 'exp', split_axis=0, concat_axis=0, tiled=True)  14.3 us
    dot_general x2, matrix products, rotate(): jnp.einsum('...ab,ca,db->...cd', blocks, paley_table, sylvester_table, pr...  5.15 us
    another operation x3, local copies, waits for them, and re-layouts, local(): jnp.stack([arrived] * lax.axis_size('hid'))  4.91 us
    all_to_all x1, starting transfers between devices, local(): lax.all_to_all(jnp.stack([arrived] * lax.axis_size('hid')), 'hid', 0, 0)  4.86 us
  transfers between devices with their start and end apart: 3, of which 2 were waited for; matrix products, arithmetic and copies ran while one was open for 10% of the time, Pallas kernels for 0%

profile of v1, /device:TPU:1, one launch (start us, length us, event | category | flops | bytes accessed | tf_op | source)
XLA Modules:
  0.0 194.4 jit_solution(18430582113617184645)
XLA Ops:
  0.7 0.9 fusion.46
  4.2 1.3 convolution_convert_fusion.1
  5.5 1.2 all_to_all.20
  6.7 48.9 %all_to_all.31 = bf16[128,4,1024]{2,1,0:T(4,128)(2,1)S(1)} all-to-all(bf16[128,4,1024]{2,1,0:T(4,128)(2,1)} %all_to_all.20), channel_id=1, replica_groups=mesh['exp'=128,'hid'=4] {'exp'}, dimensions={0} | all-to-all | bytes 2097152 | tf_op jit(solution)/shard_map/all_to_all | solution.py:74
  55.6 1.1 stack.4
  56.7 1.5 copy.44
  58.2 2.3 %stack.10 = bf16[4,512,1024]{1,2,0:T(8,128)(2,1)} broadcast(bf16[512,1024]{0,1:T(8,128)(2,1)S(1)} %copy.44), dimensions={1,2} | broadcast | bytes 5242880 | tf_op jit(solution)/shard_map/stack | solution.py:76
  60.5 4.9 %all-to-all-start.1 = ((bf16[4,512,1024]{1,2,0:T(8,128)(2,1)}), bf16[4,512,1024]{1,2,0:T(8,128)(2,1)}, u32[]{:S(2)}, u32[]{:S(2)}) async-start(bf16[4,512,1024]{1,2,0:T(8,128)(2,1)} %stack.10), calls=%async_computation.1 | async-start | bytes 8388608 | tf_op jit(solution)/shard_map/all_to_all | solution.py:76
  65.4 2.9 %reshape_squeeze.3 = bf16[192,4,1024]{2,1,0:T(4,128)(2,1)S(1)} reshape(bf16[1,192,4096]{2,1,0:T(8,128)(2,1)} %param.14) | data formatting | bytes 3145728 | tf_op jit(solution)/shard_map/reshape;squeeze | solution.py:61
  68.3 1.7 copy.45
  70.0 42.6 %all-to-all-done.1 = bf16[4,512,1024]{1,2,0:T(8,128)(2,1)} async-done(((bf16[4,512,1024]{1,2,0:T(8,128)(2,1)}), bf16[4,512,1024]{1,2,0:T(8,128)(2,1)}, u32[]{:S(2)}, u32[]{:S(2)}) %all-to-all-start.1) | async-done | bytes 4194336 | tf_op jit(solution)/shard_map/all_to_all | solution.py:76
  112.5 4.4 %all-to-all-start.2 = ((bf16[4,192,1024]{2,1,0:T(8,128)(2,1)}), bf16[4,192,1024]{2,1,0:T(8,128)(2,1)}, u32[]{:S(2)}, u32[]{:S(2)}) async-start(bf16[4,192,1024]{2,1,0:T(8,128)(2,1)} %copy.45), calls=%async_computation.2 | async-start | bytes 3145728 | tf_op jit(solution)/shard_map/all_to_all | solution.py:62
  116.9 3.3 %fusion.4 = f32[512,192]{0,1:T(8,128)S(1)} fusion(bf16[512,4096]{0,1:T(8,128)(2,1)} %bitcast.1, bf16[1,192,4096]{2,1,0:T(8,128)(2,1)S(1)} %copy-done), kind=kOutput, calls=%fused_computation.5 | convolution fusion | flops 805306368 | bytes 6160384 | tf_op jit(solution)/shard_map/dot_general | solution.py:78
  120.2 3.2 %fusion.12 = bf16[512,192]{0,1:T(8,128)(2,1)S(1)} fusion(bf16[512,4096]{0,1:T(8,128)(2,1)} %bitcast.1, bf16[1,192,4096]{2,1,0:T(8,128)(2,1)S(1)} %copy-done.5, f32[512,192]{0,1:T(8,128)S(1)} %fusion.4), kind=kOutput, calls=%fused_computation.15 | convolution fusion | flops 805896192 | bytes 6356992 | tf_op jit(solution)/shard_map/dot_general | solution.py:79
  123.4 19.3 %all_gather.3 = bf16[512,768]{0,1:T(8,128)(2,1)S(1)} all-gather(bf16[512,192]{0,1:T(8,128)(2,1)S(1)} %fusion.12), channel_id=1, replica_groups=mesh['exp'=128,'hid'=4] {'hid'}, dimensions={1}, use_global_device_ids=true | all-gather | bytes 983040 | tf_op jit(solution)/shard_map/all_gather | solution.py:81
  142.7 2.4 %convolution_convert_fusion = bf16[512,1024]{1,0:T(8,128)(2,1)S(1)} fusion(bf16[512,768]{0,1:T(8,128)(2,1)S(1)} %all_gather.3, bf16[768,1024]{1,0:T(8,128)(2,1)} %bitcast.6), kind=kOutput, calls=%fused_computation.10 | convolution fusion | flops 805830656 | bytes 3407872 | tf_op jit(solution)/shard_map/dot_general | solution.py:82
  145.1 1.2 all_to_all.24
  146.4 14.3 %all-to-all-start.3 = ((bf16[128,4,1024]{2,1,0:T(4,128)(2,1)}), bf16[128,4,1024]{2,1,0:T(4,128)(2,1)}, u32[]{:S(2)}, u32[]{:S(2)}) async-start(bf16[128,4,1024]{2,1,0:T(4,128)(2,1)} %all_to_all.24), calls=%async_computation.3 | async-start | bytes 2097152 | tf_op jit(solution)/shard_map/all_to_all | solution.py:85
  161.4 2.6 %fusion = f32[12,512,64]{1,0,2:T(8,128)S(1)} fusion(f32[12,12,1]{1,0,2:T(8,128)S(1)} %copy-done.2, f32[512,12,64]{0,2,1:T(8,128)S(1)} %bitcast.36), kind=kOutput, calls=%fused_computation.1 | convolution fusion | flops 56623104 | bytes 3146304 | tf_op jit(solution)/shard_map/...ab,ca,db->...cd/dot_general | solution.py:32
  164.1 2.5 %fusion.6 = f32[12,512,64]{1,2,0:T(8,128)S(1)} fusion(f32[12,512,64]{1,0,2:T(8,128)S(1)} %fusion), kind=kOutput, calls=%fused_computation.7 | convolution fusion | flops 302133248 | bytes 3145728 | tf_op jit(solution)/shard_map/...ab,ca,db->...cd/dot_general | solution.py:32
  166.6 2.4 %fusion.15 = bf16[1,192,768]{2,1,0:T(8,128)(2,1)} fusion(f32[512,768]{0,1:T(8,128)S(1)} %bitcast.37, s32[]{:T(128)S(6)} %select_n.25), kind=kOutput, calls=%fused_computation.16 | convolution fusion | flops 906264576 | bytes 2260996 | tf_op jit(solution)/shard_map/dot_general | solution.py:92
  169.0 21.8 %all-to-all-done.3 = bf16[128,4,1024]{2,1,0:T(4,128)(2,1)} async-done(((bf16[128,4,1024]{2,1,0:T(4,128)(2,1)}), bf16[128,4,1024]{2,1,0:T(4,128)(2,1)}, u32[]{:S(2)}, u32[]{:S(2)}) %all-to-all-start.3) | async-done | bytes 1048608 | tf_op jit(solution)/shard_map/all_to_all | solution.py:85
  190.8 1.3 all_to_all.26
  192.2 1.2 gather_fusion
  (39 shorter events, 4.3 us)
Async XLA Ops:
  0.6 116.3 %copy-start = (bf16[1,192,4096]{2,1,0:T(8,128)(2,1)S(1)}, bf16[1,192,4096]{2,1,0:T(8,128)(2,1)}, u32[]{:S(2)}) copy-start(bf16[1,192,4096]{2,1,0:T(8,128)(2,1)} %param.12) | copy-start | bytes 4718596
  60.5 52.0 %all-to-all-start.1 = ((bf16[4,512,1024]{1,2,0:T(8,128)(2,1)}), bf16[4,512,1024]{1,2,0:T(8,128)(2,1)}, u32[]{:S(2)}, u32[]{:S(2)}) async-start(bf16[4,512,1024]{1,2,0:T(8,128)(2,1)} %stack.10), calls=%async_computation.1 | async-start | bytes 8388608 | tf_op jit(solution)/shard_map/all_to_all | solution.py:76
  112.5 30.2 %all-to-all-start.2 = ((bf16[4,192,1024]{2,1,0:T(8,128)(2,1)}), bf16[4,192,1024]{2,1,0:T(8,128)(2,1)}, u32[]{:S(2)}, u32[]{:S(2)}) async-start(bf16[4,192,1024]{2,1,0:T(8,128)(2,1)} %copy.45), calls=%async_computation.2 | async-start | bytes 3145728 | tf_op jit(solution)/shard_map/all_to_all | solution.py:62
  116.9 3.3 %copy-start.5 = (bf16[1,192,4096]{2,1,0:T(8,128)(2,1)S(1)}, bf16[1,192,4096]{2,1,0:T(8,128)(2,1)}, u32[]{:S(2)}) copy-start(bf16[1,192,4096]{2,1,0:T(8,128)(2,1)} %param.13) | copy-start | bytes 4718596
  146.4 14.5 %copy-start.3 = (f32[32,8]{0,1:T(8,128)S(1)}, f32[32,8]{0,1:T(8,128)}, u32[]{:S(2)}) copy-start(f32[32,8]{0,1:T(8,128)} %param.10) | copy-start | bytes 3076
  146.4 14.6 %copy-start.4 = (s32[1,768]{1,0:T(1,128)S(1)}, s32[1,768]{1,0:T(1,128)}, u32[]{:S(2)}) copy-start(s32[1,768]{1,0:T(1,128)} %param.11) | copy-start | bytes 9220
  146.4 44.4 %all-to-all-start.3 = ((bf16[128,4,1024]{2,1,0:T(4,128)(2,1)}), bf16[128,4,1024]{2,1,0:T(4,128)(2,1)}, u32[]{:S(2)}, u32[]{:S(2)}) async-start(bf16[128,4,1024]{2,1,0:T(4,128)(2,1)} %all_to_all.24), calls=%async_computation.3 | async-start | bytes 2097152 | tf_op jit(solution)/shard_map/all_to_all | solution.py:85
  160.7 0.7 copy-start.2
  192.2 1.6 copy-start.1
